TPU v7x, 256 devices: a whole 4x4x8 slice. The times are simulated.
256 devices in a mesh: expert: 64 (over z, y, x_hi), tensor: 4 (over x_lo, core).
Axes of the slice: x: 4 (x_hi: 2, x_lo: 2; x = x_hi * 2 + x_lo), y: 4, z: 8, core: 2. Of those that a mesh axis runs over, the one named last changes fastest.
Arguments:
- attn_partial: bfloat16 [4, 8192, 4096], P('tensor', 'expert'), may hold values from -4 to 4
- residual: bfloat16 [8192, 4096], P('expert', 'tensor'), may hold values from -40 to 40
- norm_gain: float32 [4096], P('tensor'), may hold values from 0.1 to 1.9
- expert_ids: int32 [8192, 4], P('expert'), may hold values from 0 to 63, all different within a row; in each aligned block of 128 rows (0 to 127, 128 to 255, ...) at most 10 rows name the same one
- route_weight: float32 [8192, 4], P('expert'), may hold values from 0.1 to 1
- w_in: bfloat16 [64, 4096, 2048], P('expert', 'tensor'), may hold values from -0.09375 to 0.09375
- w_down: bfloat16 [64, 1024, 4096], P('expert', None, 'tensor'), may hold values from -0.1875 to 0.1875
Outputs:
- layer_out: bfloat16 [8192, 4096], P('expert', 'tensor')
Inputs may be any that keep to these rules, and one draw needn't show every extreme that they name: `expert_ids`: in each aligned block of 128 rows (the tokens of one index of expert) no expert is named by more than 10 rows, a bound that some block reaches. A row names 4 different experts.
All inputs are finite; a program needn't handle non-finite values.
Results may differ from a plain program's by a relative error of at most 0.01.
Values may be sent and summed in bfloat16 or wider, within the bound.
No kernel may reach another device: no remote copies, remote signals or barrier semaphores. Data moves between devices by JAX's collectives and lax.ppermute only.
A program may use at most 64 MiB of HBM per device.

v0:
```python
import jax
import jax.numpy as jnp
from jax import lax
from jax.sharding import PartitionSpec as P


def body(attn_partial, residual, norm_gain, expert_ids, route_weight, w_in, w_down):
    token_count = expert_ids.shape[0]
    topk_count = expert_ids.shape[1]
    feature_local = residual.shape[1]
    feature_count = feature_local * lax.axis_size("tensor")
    hidden_width = w_down.shape[1]
    expert_count = lax.axis_size("expert")
    capacity = 5 * token_count * topk_count // (4 * expert_count)
    attention = lax.psum_scatter(
        attn_partial[0].astype(jnp.float32).astype(jnp.bfloat16),
        "tensor",
        scatter_dimension=1,
        tiled=True,
    ).astype(jnp.float32)
    stream = residual.astype(jnp.float32) + attention
    squares = lax.psum(jnp.sum(stream * stream, axis=1), "tensor")
    inverse = lax.rsqrt(squares / feature_count + 1e-06)[:, None]
    normed = stream * inverse * norm_gain[None, :]
    rows = normed.astype(jnp.bfloat16)
    flat_ids = expert_ids.reshape(-1)
    one_hot = (flat_ids[:, None] == jnp.arange(expert_count, dtype=jnp.int32)[None, :]).astype(
        jnp.int32
    )
    earlier = jnp.cumsum(one_hot, axis=0) - one_hot
    slot_index = jnp.sum(earlier * one_hot, axis=1)
    positions = (flat_ids * capacity + slot_index).reshape(token_count, topk_count)
    places = jnp.arange(expert_count * capacity, dtype=jnp.int32)
    matches = positions[None, :, :] == places[:, None, None]
    dispatch = jnp.any(matches, axis=2)
    sent_rows = jnp.dot(dispatch.astype(jnp.bfloat16), rows, preferred_element_type=jnp.float32)
    sent_rows = sent_rows.astype(jnp.bfloat16).reshape(expert_count, capacity, feature_local)
    weights_table = jnp.sum(jnp.where(matches, route_weight[None, :, :], 0.0), axis=2).T
    in_rows = lax.all_to_all(sent_rows, "expert", split_axis=0, concat_axis=0, tiled=True)
    source_count = in_rows.shape[0]
    item_count = in_rows.shape[1]
    row_total = source_count * item_count
    flat_rows = in_rows.reshape(row_total, feature_local)
    partial_value = jnp.dot(flat_rows, w_in[0], preferred_element_type=jnp.float32)
    total = lax.psum_scatter(
        partial_value.astype(jnp.bfloat16), "tensor", scatter_dimension=0, tiled=True
    ).astype(jnp.float32)
    hidden = (jax.nn.silu(total[:, :hidden_width]) * total[:, hidden_width:]).astype(jnp.bfloat16)
    hidden = lax.all_gather(hidden, "tensor", axis=0, tiled=True)
    produced = jnp.dot(hidden, w_down[0], preferred_element_type=jnp.float32).astype(jnp.bfloat16)
    results = produced.reshape(source_count, item_count, feature_local)
    returned = lax.all_to_all(results, "expert", split_axis=0, concat_axis=0, tiled=True)
    routed = jnp.dot(
        weights_table,
        returned.reshape(expert_count * capacity, feature_local).astype(jnp.float32),
        precision=lax.Precision.HIGHEST,
    )
    return (stream + routed).astype(jnp.bfloat16)


def solution(mesh):
    in_specs = (
        P("tensor", "expert", None),
        P("expert", "tensor"),
        P("tensor"),
        P("expert", None),
        P("expert", None),
        P("expert", "tensor", None),
        P("expert", None, "tensor"),
    )
    out_specs = P("expert", "tensor")
    return jax.shard_map(body, mesh=mesh, in_specs=in_specs, out_specs=out_specs, check_vma=False)
```

profile of v0, /device:TPU:32, one launch (start us, length us, event | category | flops | bytes accessed | tf_op | source)
XLA Modules:
  0.0 259.2 jit_solution(11429051957058724072)
XLA Ops:
  6.6 0.7 reduce-scatter.3.cloned.1.call-update
  7.3 0.8 copy.22
  8.3 1.2 reduce-window.6
  9.5 0.2 slice_reduce_fusion
  10.1 0.2 fusion.10
  10.3 24.9 %reduce-scatter.3.cloned.1.call-done = bf16[128,1024]{1,0:T(8,128)(2,1)} async-done(((bf16[128,4096]{1,0:T(8,128)(2,1)}), bf16[128,1024]{1,0:T(8,128)(2,1)}) %reduce-scatter.3.cloned.1.call-update) | async-done | bytes 262160 | tf_op jit(solution)/shard_map/reduce_scatter | solution.py:15
  35.2 1.1 multiply_reduce_fusion
  36.4 6.4 %psum.7 = f32[128]{0:T(128)S(1)} all-reduce(f32[128]{0:T(128)S(1)} %multiply_reduce_fusion), channel_id=1, replica_groups=mesh['expert'=64,'tensor'=4] {'tensor'}, use_global_device_ids=true, to_apply=%region_7.8 | all-reduce | flops 128 | bytes 1024 | tf_op jit(solution)/shard_map/psum | solution.py:22
  42.8 1.6 convolution_convert_fusion
  44.4 1.6 reshape.40
  46.0 64.5 %all_to_all.10 = bf16[64,10,1024]{2,1,0:T(8,128)(2,1)} all-to-all(bf16[64,10,1024]{2,1,0:T(8,128)(2,1)} %reshape.40), channel_id=1, replica_groups=mesh['expert'=64,'tensor'=4] {'expert'}, dimensions={0} | all-to-all | bytes 2621440 | tf_op jit(solution)/shard_map/all_to_all | solution.py:39
  110.5 2.6 reshape.41
  113.0 6.3 %fusion.2 = bf16[640,2048]{1,0:T(8,128)(2,1)} fusion(bf16[640,1024]{1,0:T(8,128)(2,1)S(1)} %reshape.41, bf16[1,1024,2048]{2,1,0:T(8,128)(2,1)} %param.12), kind=kOutput, calls=%fused_computation.2 | convolution fusion | flops 2685665280 | bytes 8126464 | tf_op jit(solution)/shard_map/dot_general | solution.py:44
  119.5 29.7 %reduce-scatter.5.cloned.1.call-done = bf16[160,2048]{1,0:T(8,128)(2,1)} async-done(((bf16[640,2048]{1,0:T(8,128)(2,1)}), bf16[160,2048]{1,0:T(8,128)(2,1)}) %reduce-scatter.5.cloned.1.call-update) | async-done | bytes 655376 | tf_op jit(solution)/shard_map/reduce_scatter | solution.py:45
  149.1 1.2 convert_element_type.45
  150.4 0.9 fusion.12
  151.3 26.1 %all-gather.2.cloned.1.call-done = bf16[640,1024]{1,0:T(8,128)(2,1)} async-done(((bf16[160,1024]{1,0:T(8,128)(2,1)}), bf16[640,1024]{1,0:T(8,128)(2,1)}) %all-gather.2.cloned.1.call-update) | async-done | bytes 1310736 | tf_op jit(solution)/shard_map/all_gather | solution.py:49
  177.5 2.8 %fusion.7 = bf16[640,1024]{1,0:T(8,128)(2,1)S(1)} fusion(bf16[640,1024]{1,0:T(8,128)(2,1)} %all-gather.2.cloned.1.call-done, bf16[1,1024,1024]{2,1,0:T(8,128)(2,1)S(1)} %copy-done), kind=kOutput, calls=%fused_computation.5 | convolution fusion | flops 1342832640 | bytes 4718592 | tf_op jit(solution)/shard_map/dot_general | solution.py:50
  180.3 1.5 reshape.42
  181.8 12.9 %all-to-all-start.1 = ((bf16[64,10,1024]{2,1,0:T(8,128)(2,1)}), bf16[64,10,1024]{2,1,0:T(8,128)(2,1)}, u32[]{:S(2)}, u32[]{:S(2)}) async-start(bf16[64,10,1024]{2,1,0:T(8,128)(2,1)} %reshape.42), calls=%async_computation.3 | async-start | bytes 4194304 | tf_op jit(solution)/shard_map/all_to_all | solution.py:52
  194.8 0.9 select_reduce_fusion
  195.6 51.7 %all-to-all-done.1 = bf16[64,10,1024]{2,1,0:T(8,128)(2,1)} async-done(((bf16[64,10,1024]{2,1,0:T(8,128)(2,1)}), bf16[64,10,1024]{2,1,0:T(8,128)(2,1)}, u32[]{:S(2)}, u32[]{:S(2)}) %all-to-all-start.1) | async-done | bytes 1310752 | tf_op jit(solution)/shard_map/all_to_all | solution.py:52
  247.4 2.6 reshape.43
  250.0 2.7 %fusion.11 = bf16[128,1024]{1,0:T(8,128)(2,1)} fusion(f32[640,128]{1,0:T(8,128)} %select_reduce_fusion, bf16[640,1024]{1,0:T(8,128)(2,1)S(1)} %reshape.43, bf16[128,1024]{1,0:T(8,128)(2,1)} %reduce-scatter.3.cloned.1.call-done, bf16[128,1024]{1,0:T(8,128)(2,1)} %param.8), kind=kOutput, calls=%fused_computation.11 | convolution fusion | flops 1007288320 | bytes 2424832 | tf_op jit(solution)/shard_map/dot_general | solution.py:53
  (25 shorter events, 0.7 us)
Async XLA Ops:
  6.5 170.9 %copy-start = (bf16[1,1024,1024]{2,1,0:T(8,128)(2,1)S(1)}, bf16[1,1024,1024]{2,1,0:T(8,128)(2,1)}, u32[]{:S(2)}) copy-start(bf16[1,1024,1024]{2,1,0:T(8,128)(2,1)} %param.13) | copy-start | bytes 6291460
  6.5 3.6 %copy-start.2 = (s32[128,4]{0,1:T(4,128)S(1)}, s32[128,4]{0,1:T(4,128)}, u32[]{:S(2)}) copy-start(s32[128,4]{0,1:T(4,128)} %param.10) | copy-start | bytes 6148
  6.5 28.7 %copy-start.1 = (bf16[128,1024]{1,0:T(8,128)(2,1)S(1)}, bf16[128,1024]{1,0:T(8,128)(2,1)}, u32[]{:S(2)}) copy-start(bf16[128,1024]{1,0:T(8,128)(2,1)} %param.8) | copy-start | bytes 786436
  6.5 28.7 %reduce-scatter.3.cloned.1.call-start = ((), (), s32[]{:S(2)}) async-start(), calls=%async_computation.4 | async-start | bytes 1310720 | tf_op jit(solution)/shard_map/reduce_scatter | solution.py:15
  6.5 36.2 %copy-start.3 = (f32[1024]{0:T(1024)S(1)}, f32[1024]{0:T(1024)}, u32[]{:S(2)}) copy-start(f32[1024]{0:T(1024)} %param.9) | copy-start | bytes 12292
  7.3 141.9 %reduce-scatter.5.cloned.1.call-start = ((), (), s32[]{:S(2)}) async-start(), calls=%async_computation.5 | async-start | bytes 3276800 | tf_op jit(solution)/shard_map/reduce_scatter | solution.py:45
  119.4 58.0 %all-gather.2.cloned.1.call-start = ((), (), s32[]{:S(2)}) async-start(), calls=%async_computation.6 | async-start | bytes 1638400 | tf_op jit(solution)/shard_map/all_gather | solution.py:49
  181.8 12.9 %copy-start.4 = (f32[128,4]{0,1:T(4,128)S(1)}, f32[128,4]{0,1:T(4,128)}, u32[]{:S(2)}) copy-start(f32[128,4]{0,1:T(4,128)} %param.11) | copy-start | bytes 6148
  181.8 65.6 %all-to-all-start.1 = ((bf16[64,10,1024]{2,1,0:T(8,128)(2,1)}), bf16[64,10,1024]{2,1,0:T(8,128)(2,1)}, u32[]{:S(2)}, u32[]{:S(2)}) async-start(bf16[64,10,1024]{2,1,0:T(8,128)(2,1)} %reshape.42), calls=%async_computation.3 | async-start | bytes 4194304 | tf_op jit(solution)/shard_map/all_to_all | solution.py:52
Sparse Core Ops, SparseCore 0:
  9.9 25.3 reduce-scatter.2
  119.5 29.5 reduce-scatter.4
  151.5 25.9 all-gather.1
where the time goes:
time: 260 us; the launch traced here: 259 us
  waiting for transfers between devices  133 us (51%)
  blocking collectives  70.9 us (27%)
  matrix products  13.5 us (5%)
  between operations  13.2 us (5%)
  starting transfers between devices  13 us (5%)
  local copies, waits for them, and re-layouts  9.65 us (4%)
  other arithmetic  5.72 us (2%)
    all_to_all x1, blocking collectives, body(): lax.all_to_all(sent_rows, 'expert', split_axis=0, concat_axis=0, tiled=True)  64.5 us
    all_to_all x1, waiting for transfers between devices, body(): lax.all_to_all(results, 'expert', split_axis=0, concat_axis=0, tiled=True)  51.7 us
    reduce_scatter x1, waiting for transfers between devices, body(): lax.psum_scatter(partial_value.astype(jnp.bfloat16), 'tensor', scatter_di...  29.7 us
    all_gather x1, waiting for transfers between devices, body(): hidden = lax.all_gather(hidden, 'tensor', axis=0, tiled=True)  26.1 us
    reduce_scatter x1, waiting for transfers between devices, body(): lax.psum_scatter(attn_partial[0].astype(jnp.float32).astype(jnp.bfloat16)...  24.9 us
    all_to_all x1, starting transfers between devices, body(): lax.all_to_all(results, 'expert', split_axis=0, concat_axis=0, tiled=True)  12.9 us
    psum x1, blocking collectives, body(): squares = lax.psum(jnp.sum(stream * stream, axis=1), 'tensor')  6.38 us
    dot_general x1, matrix products, body(): jnp.dot(flat_rows, w_in[0], preferred_element_type=jnp.float32)  6.35 us
  transfers between devices with their start and end apart: 4, of which 4 were waited for; matrix products, arithmetic and copies ran while one was open for 1% of the time, Pallas kernels for 0%

commit v1 on v0

--- a/solution.py
+++ b/solution.py
@@ -46,7 +46,8 @@
         partial_value.astype(jnp.bfloat16), "tensor", scatter_dimension=0, tiled=True
     ).astype(jnp.float32)
     hidden = (jax.nn.silu(total[:, :hidden_width]) * total[:, hidden_width:]).astype(jnp.bfloat16)
-    hidden = lax.all_gather(hidden, "tensor", axis=0, tiled=True)
+    stack = jnp.stack([hidden] * lax.axis_size("tensor"))
+    hidden = jnp.concatenate(lax.all_to_all(stack, "tensor", 0, 0), axis=0)
     produced = jnp.dot(hidden, w_down[0], preferred_element_type=jnp.float32).astype(jnp.bfloat16)
     results = produced.reshape(source_count, item_count, feature_local)
     returned = lax.all_to_all(results, "expert", split_axis=0, concat_axis=0, tiled=True)

time: 260 us -> 251 us (0.965)
  waiting for transfers between devices: 133 us -> 106 us
  blocking collectives: 70.9 us -> 90.6 us
    all_gather x1 -> x0, waiting for transfers between devices: 26.1 us -> none  [body(): hidden = lax.all_gather(hidden, 'tensor', axis=0, tiled=True)]
    all_to_all x0 -> x1, blocking collectives: none -> 19.7 us  [body(): hidden = jnp.concatenate(lax.all_to_all(stack, 'tensor', 0, 0), axis=0)]
  transfers between devices with their start and end apart: 4 -> 3, of which waited for: 4 -> 3; matrix products, arithmetic and copies ran while one was open for 1% -> 2% of each run, Pallas kernels for 0% -> 0%
where the time goes in v1:
time: 251 us; the launch traced here: 250 us
  waiting for transfers between devices  106 us (42%)
  blocking collectives  90.6 us (36%)
  between operations  13.5 us (5%)
  starting transfers between devices  13 us (5%)
  matrix products  12.2 us (5%)
  local copies, waits for them, and re-layouts  9.81 us (4%)
  other arithmetic  4.96 us (2%)
    all_to_all x1, blocking collectives, body(): lax.all_to_all(sent_rows, 'expert', split_axis=0, concat_axis=0, tiled=True)  64.5 us
    all_to_all x1, waiting for transfers between devices, body(): lax.all_to_all(results, 'expert', split_axis=0, concat_axis=0, tiled=True)  50.5 us
    reduce_scatter x1, waiting for transfers between devices, body(): lax.psum_scatter(partial_value.astype(jnp.bfloat16), 'tensor', scatter_di...  29.7 us
    reduce_scatter x1, waiting for transfers between devices, body(): lax.psum_scatter(attn_partial[0].astype(jnp.float32).astype(jnp.bfloat16)...  24.9 us
    all_to_all x1, blocking collectives, body(): hidden = jnp.concatenate(lax.all_to_all(stack, 'tensor', 0, 0), axis=0)  19.7 us
    all_to_all x1, starting transfers between devices, body(): lax.all_to_all(results, 'expert', split_axis=0, concat_axis=0, tiled=True)  12.9 us
    psum x1, blocking collectives, body(): squares = lax.psum(jnp.sum(stream * stream, axis=1), 'tensor')  6.38 us
    dot_general x1, matrix products, body(): jnp.dot(flat_rows, w_in[0], preferred_element_type=jnp.float32)  6.35 us
  transfers between devices with their start and end apart: 3, of which 3 were waited for; matrix products, arithmetic and copies ran while one was open for 2% of the time, Pallas kernels for 0%

profile of v1, /device:TPU:32, one launch (start us, length us, event | category | flops | bytes accessed | tf_op | source)
XLA Modules:
  0.0 249.9 jit_solution(17327919110416782305)
XLA Ops:
  6.6 0.7 reduce-scatter.3.cloned.1.call-update
  7.3 0.8 copy.22
  8.3 1.2 reduce-window.6
  9.5 0.2 slice_reduce_fusion
  10.1 0.2 fusion.10
  10.3 24.9 %reduce-scatter.3.cloned.1.call-done = bf16[128,1024]{1,0:T(8,128)(2,1)} async-done(((bf16[128,4096]{1,0:T(8,128)(2,1)}), bf16[128,1024]{1,0:T(8,128)(2,1)}) %reduce-scatter.3.cloned.1.call-update) | async-done | bytes 262160 | tf_op jit(solution)/shard_map/reduce_scatter | solution.py:15
  35.2 1.1 multiply_reduce_fusion
  36.4 6.4 %psum.7 = f32[128]{0:T(128)S(1)} all-reduce(f32[128]{0:T(128)S(1)} %multiply_reduce_fusion), channel_id=1, replica_groups=mesh['expert'=64,'tensor'=4] {'tensor'}, use_global_device_ids=true, to_apply=%region_7.8 | all-reduce | flops 128 | bytes 1024 | tf_op jit(solution)/shard_map/psum | solution.py:22
  42.8 1.6 convolution_convert_fusion
  44.4 1.6 reshape.45
  46.0 64.5 %all_to_all.15 = bf16[64,10,1024]{2,1,0:T(8,128)(2,1)} all-to-all(bf16[64,10,1024]{2,1,0:T(8,128)(2,1)} %reshape.45), channel_id=1, replica_groups=mesh['expert'=64,'tensor'=4] {'expert'}, dimensions={0} | all-to-all | bytes 2621440 | tf_op jit(solution)/shard_map/all_to_all | solution.py:39
  110.5 2.6 %reshape.46 = bf16[640,1024]{1,0:T(8,128)(2,1)S(1)} reshape(bf16[64,10,1024]{2,1,0:T(8,128)(2,1)} %all_to_all.15) | data formatting | bytes 2621440 | tf_op jit(solution)/shard_map/reshape | solution.py:43
  113.0 6.3 %fusion.2 = bf16[640,2048]{1,0:T(8,128)(2,1)} fusion(bf16[640,1024]{1,0:T(8,128)(2,1)S(1)} %reshape.46, bf16[1,1024,2048]{2,1,0:T(8,128)(2,1)} %param.12), kind=kOutput, calls=%fused_computation.2 | convolution fusion | flops 2685665280 | bytes 8126464 | tf_op jit(solution)/shard_map/dot_general | solution.py:44
  119.4 29.7 %reduce-scatter.5.cloned.1.call-done = bf16[160,2048]{1,0:T(8,128)(2,1)} async-done(((bf16[640,2048]{1,0:T(8,128)(2,1)}), bf16[160,2048]{1,0:T(8,128)(2,1)}) %reduce-scatter.5.cloned.1.call-update) | async-done | bytes 655376 | tf_op jit(solution)/shard_map/reduce_scatter | solution.py:45
  149.1 1.2 convert_element_type.45
  150.4 0.2 fusion.12
  150.7 19.7 %all_to_all.16 = bf16[4,160,1024]{2,1,0:T(8,128)(2,1)S(1)} all-to-all(bf16[4,160,1024]{2,1,0:T(8,128)(2,1)S(1)} %stack.2), channel_id=1, replica_groups=mesh['expert'=64,'tensor'=4] {'tensor'}, dimensions={0} | all-to-all | bytes 2621440 | tf_op jit(solution)/shard_map/all_to_all | solution.py:50
  170.4 1.5 fusion.7
  172.0 1.5 reshape.48
  173.5 12.9 %all-to-all-start.2 = ((bf16[64,10,1024]{2,1,0:T(8,128)(2,1)}), bf16[64,10,1024]{2,1,0:T(8,128)(2,1)}, u32[]{:S(2)}, u32[]{:S(2)}) async-start(bf16[64,10,1024]{2,1,0:T(8,128)(2,1)} %reshape.48), calls=%async_computation.4 | async-start | bytes 4194304 | tf_op jit(solution)/shard_map/all_to_all | solution.py:53
  186.4 0.9 select_reduce_fusion
  187.3 50.5 %all-to-all-done.2 = bf16[64,10,1024]{2,1,0:T(8,128)(2,1)} async-done(((bf16[64,10,1024]{2,1,0:T(8,128)(2,1)}), bf16[64,10,1024]{2,1,0:T(8,128)(2,1)}, u32[]{:S(2)}, u32[]{:S(2)}) %all-to-all-start.2) | async-done | bytes 1310752 | tf_op jit(solution)/shard_map/all_to_all | solution.py:53
  237.8 2.6 %reshape.49 = bf16[640,1024]{1,0:T(8,128)(2,1)S(1)} reshape(bf16[64,10,1024]{2,1,0:T(8,128)(2,1)} %all-to-all-done.2) | data formatting | bytes 2621440 | tf_op jit(solution)/shard_map/reshape | solution.py:56
  240.4 2.7 %fusion.11 = bf16[128,1024]{1,0:T(8,128)(2,1)} fusion(f32[640,128]{1,0:T(8,128)} %select_reduce_fusion, bf16[640,1024]{1,0:T(8,128)(2,1)S(1)} %reshape.49, bf16[128,1024]{1,0:T(8,128)(2,1)} %reduce-scatter.3.cloned.1.call-done, bf16[128,1024]{1,0:T(8,128)(2,1)} %param.8), kind=kOutput, calls=%fused_computation.11 | convolution fusion | flops 1007288320 | bytes 2424832 | tf_op jit(solution)/shard_map/dot_general | solution.py:54
  (24 shorter events, 0.8 us)
Async XLA Ops:
  6.5 163.9 %copy-start = (bf16[1,1024,1024]{2,1,0:T(8,128)(2,1)S(1)}, bf16[1,1024,1024]{2,1,0:T(8,128)(2,1)}, u32[]{:S(2)}) copy-start(bf16[1,1024,1024]{2,1,0:T(8,128)(2,1)} %param.13) | copy-start | bytes 6291460
  6.5 3.6 %copy-start.2 = (s32[128,4]{0,1:T(4,128)S(1)}, s32[128,4]{0,1:T(4,128)}, u32[]{:S(2)}) copy-start(s32[128,4]{0,1:T(4,128)} %param.10) | copy-start | bytes 6148
  6.5 28.7 %copy-start.1 = (bf16[128,1024]{1,0:T(8,128)(2,1)S(1)}, bf16[128,1024]{1,0:T(8,128)(2,1)}, u32[]{:S(2)}) copy-start(bf16[128,1024]{1,0:T(8,128)(2,1)} %param.8) | copy-start | bytes 786436
  6.5 28.7 %reduce-scatter.3.cloned.1.call-start = ((), (), s32[]{:S(2)}) async-start(), calls=%async_computation.5 | async-start | bytes 1310720 | tf_op jit(solution)/shard_map/reduce_scatter | solution.py:15
  6.5 36.2 %copy-start.3 = (f32[1024]{0:T(1024)S(1)}, f32[1024]{0:T(1024)}, u32[]{:S(2)}) copy-start(f32[1024]{0:T(1024)} %param.9) | copy-start | bytes 12292
  7.3 141.9 %reduce-scatter.5.cloned.1.call-start = ((), (), s32[]{:S(2)}) async-start(), calls=%async_computation.6 | async-start | bytes 3276800 | tf_op jit(solution)/shard_map/reduce_scatter | solution.py:45
  173.5 12.9 %copy-start.4 = (f32[128,4]{0,1:T(4,128)S(1)}, f32[128,4]{0,1:T(4,128)}, u32[]{:S(2)}) copy-start(f32[128,4]{0,1:T(4,128)} %param.11) | copy-start | bytes 6148
  173.5 64.3 %all-to-all-start.2 = ((bf16[64,10,1024]{2,1,0:T(8,128)(2,1)}), bf16[64,10,1024]{2,1,0:T(8,128)(2,1)}, u32[]{:S(2)}, u32[]{:S(2)}) async-start(bf16[64,10,1024]{2,1,0:T(8,128)(2,1)} %reshape.48), calls=%async_computation.4 | async-start | bytes 4194304 | tf_op jit(solution)/shard_map/all_to_all | solution.py:53
Sparse Core Ops, SparseCore 0:
  9.9 25.3 reduce-scatter.2
  119.5 29.5 reduce-scatter.4
